TPU v7x, 256 devices: a whole 4x4x8 slice. The times are simulated.
256 devices in a mesh: group: 16 (over y_hi, x, core), leaf: 16 (over y_lo, z).
Axes of the slice: x: 4, y: 4 (y_hi: 2, y_lo: 2; y = y_hi * 2 + y_lo), z: 8, core: 2. Of those that a mesh axis runs over, the one named last changes fastest.
Arguments:
- leaf_mass: bfloat16 [256, 512, 512], P(('group', 'leaf')), may hold values from -23 to 23, as said below
- leaf_damp: bfloat16 [256, 512, 512], P(('group', 'leaf')), may hold values from -12 to 12, as said below
- mass_coupling: bfloat16 [256, 512, 1536], P(('group', 'leaf')), may hold values from -6 to 6
- damp_coupling: bfloat16 [256, 512, 1536], P(('group', 'leaf')), may hold values from -6 to 6
- leaf_modes: bfloat16 [256, 512, 1536], P(('group', 'leaf')), may hold values from -0.15625 to 0.15625
- interface_blocks: int32 [256, 12], P(('group', 'leaf')), may hold values from 0 to 11, each once within a row
- mid_modes: bfloat16 [16, 1536, 256], P('group', 'leaf'), may hold values from -0.15625 to 0.15625
- mid_constraint: bfloat16 [16, 1536, 1024], P('group', 'leaf'), may hold values from -0.109375 to 0.109375
Outputs:
- coupling_mass: float32 [256, 512, 256], P(('group', 'leaf'))
- coupling_damp: float32 [256, 512, 256], P(('group', 'leaf'))
- modal_mass: float32 [16, 256, 1280], P('group', 'leaf')
- modal_damp: float32 [16, 256, 1280], P('group', 'leaf')
- root_mass: float32 [1024, 1024], P(('group', 'leaf'))
- root_damp: float32 [1024, 1024], P(('group', 'leaf'))
Inputs may be any that keep to these rules, and one draw needn't show every extreme that they name: `interface_blocks`: each row is a permutation of 0 to 11. `leaf_mass`: each leaf's block is symmetric. `leaf_damp`: each leaf's block is symmetric.
All inputs are finite; a program needn't handle non-finite values.
Results may differ from a plain program's by a relative error of at most 0.0049.
Values may be sent and summed in bfloat16 or wider, within the bound.
No kernel may reach another device: no remote copies, remote signals or barrier semaphores. Data moves between devices by JAX's collectives and lax.ppermute only.
A program may use at most 128 MiB of HBM per device.

v0:
```python
import jax
import jax.numpy as jnp
from jax import lax
from jax.sharding import PartitionSpec as P


def to_middle(stacked, onehot, block_count, block_size):
    rows_total, width_total = stacked.shape
    moved = jnp.einsum(
        "lbk,bj->ljk",
        stacked.reshape(rows_total, block_count, block_size),
        onehot,
        preferred_element_type=jnp.float32,
    )
    return moved.astype(jnp.bfloat16).reshape(rows_total, width_total)


def left_product(first_operand, second_operand):
    return lax.dot_general(
        first_operand, second_operand, (((0,), (0,)), ((), ())), preferred_element_type=jnp.float32
    )


def body(
    leaf_mass,
    leaf_damp,
    mass_coupling,
    damp_coupling,
    leaf_modes,
    interface_blocks,
    mid_modes,
    mid_constraint,
):
    leaf_order = leaf_mass.shape[1]
    block_count = interface_blocks.shape[1]
    sep_width = leaf_modes.shape[2]
    block_size = sep_width // block_count
    mode_count = mid_modes.shape[2]
    root_width = mid_constraint.shape[2]
    basis_width = mode_count + root_width
    leaf_count = lax.axis_size("leaf")
    group_count = lax.axis_size("group")
    onehot = (
        interface_blocks[0][:, None] == jnp.arange(block_count, dtype=jnp.int32)[None, :]
    ).astype(jnp.bfloat16)
    placed = to_middle(
        jnp.concatenate([leaf_modes[0], mass_coupling[0], damp_coupling[0]], axis=0),
        onehot,
        block_count,
        block_size,
    )
    constraint = placed[:leaf_order]
    sides = placed[leaf_order:].astype(jnp.float32)
    product = jnp.dot(
        jnp.concatenate([leaf_mass[0], leaf_damp[0]], axis=0),
        constraint,
        preferred_element_type=jnp.float32,
    )
    half_work = (0.5 * product + sides).astype(jnp.bfloat16)
    full_work = (product + sides).astype(jnp.bfloat16)
    basis_rows = jnp.concatenate([mid_modes[0], mid_constraint[0]], axis=1)
    mode_basis = lax.all_gather(basis_rows, "leaf", axis=0, tiled=True)
    left_sum = jnp.dot(constraint, mode_basis, preferred_element_type=jnp.float32)
    right_sum = jnp.dot(half_work, mode_basis, preferred_element_type=jnp.float32)
    coupling = jnp.dot(full_work, mode_basis[:, :mode_count], preferred_element_type=jnp.float32)
    left_part = left_sum.astype(jnp.bfloat16)
    right_part = right_sum.astype(jnp.bfloat16)
    right_mass = right_part[:leaf_order]
    right_damp = right_part[leaf_order:]

    def projected_rows(first_row, amount, first_col):
        left_rows = lax.dynamic_slice_in_dim(left_part, first_row, amount, 1)
        right_rows = lax.dynamic_slice_in_dim(right_part, first_row, amount, 1)
        left_cols = left_part[:, first_col:]
        mass_term = left_product(left_rows, right_mass[:, first_col:]) + left_product(
            right_rows[:leaf_order], left_cols
        )
        damp_term = left_product(left_rows, right_damp[:, first_col:]) + left_product(
            right_rows[leaf_order:], left_cols
        )
        return jnp.concatenate([mass_term, damp_term], axis=1)

    modal_part = lax.psum_scatter(
        projected_rows(jnp.int32(0), mode_count, 0), "leaf", scatter_dimension=0, tiled=True
    )
    device_count = group_count * leaf_count
    core_odd = lax.axis_index("group") % 2 == 1
    left_root = left_part[:, mode_count:]
    mass_root = right_mass[:, mode_count:]
    damp_root = right_damp[:, mode_count:]
    own_right = jnp.where(core_odd, damp_root, mass_root)
    other_right = jnp.where(core_odd, mass_root, damp_root)
    partner = lax.ppermute(
        jnp.concatenate([left_root, other_right], axis=0),
        "group",
        [(index, index ^ 1) for index in range(group_count)],
    )
    left_pair = jnp.concatenate([left_root, partner[:leaf_order]], axis=0)
    right_pair = jnp.concatenate([own_right, partner[leaf_order:]], axis=0)
    root_rows = left_product(left_pair, right_pair) + left_product(right_pair, left_pair)
    root_recv = lax.all_to_all(
        root_rows.reshape(device_count, root_width // device_count, root_width).astype(
            jnp.bfloat16
        ),
        ("group", "leaf"),
        0,
        0,
        tiled=True,
    )
    root_part = jnp.sum(
        root_recv.reshape(
            group_count // 2, 2, leaf_count, root_width // device_count, root_width
        ).astype(jnp.float32),
        axis=(0, 2),
    )
    return (
        coupling[:leaf_order][None],
        coupling[leaf_order:][None],
        modal_part[:, :basis_width][None],
        modal_part[:, basis_width:][None],
        root_part[0],
        root_part[1],
    )


def solution(mesh):
    return jax.shard_map(
        body,
        mesh=mesh,
        in_specs=(
            P(("group", "leaf"), None, None),
            P(("group", "leaf"), None, None),
            P(("group", "leaf"), None, None),
            P(("group", "leaf"), None, None),
            P(("group", "leaf"), None, None),
            P(("group", "leaf"), None),
            P("group", "leaf", None),
            P("group", "leaf", None),
        ),
        out_specs=(
            P(("group", "leaf"), None, None),
            P(("group", "leaf"), None, None),
            P("group", "leaf", None),
            P("group", "leaf", None),
            P(("group", "leaf"), None),
            P(("group", "leaf"), None),
        ),
        check_vma=False,
    )
```

profile of v0, /device:TPU:4, one launch (start us, length us, event | category | flops | bytes accessed | tf_op | source)
XLA Modules:
  0.0 214.4 jit_solution(18022343488197545717)
XLA Ops:
  7.2 1.6 pad_maximum_fusion.8
  8.9 1.7 copy.26
  10.7 3.0 %copy.29 = bf16[512,12,128]{2,1,0:T(8,128)(2,1)} copy(bf16[512,12,128]{0,2,1:T(8,128)(2,1)S(1)} %bitcast.40) | data formatting | bytes 3145728 | tf_op jit(solution)/shard_map/concatenate | solution.py:47
  13.7 0.7 copy.25
  14.4 3.0 %copy.28 = bf16[512,12,128]{2,1,0:T(8,128)(2,1)} copy(bf16[512,12,128]{0,2,1:T(8,128)(2,1)S(1)} %bitcast.41) | data formatting | bytes 3145728 | tf_op jit(solution)/shard_map/concatenate | solution.py:47
  17.5 0.7 copy.24
  18.2 3.0 %copy.27 = bf16[512,12,128]{2,1,0:T(8,128)(2,1)} copy(bf16[512,12,128]{0,2,1:T(8,128)(2,1)S(1)} %bitcast.42) | data formatting | bytes 3145728 | tf_op jit(solution)/shard_map/concatenate | solution.py:47
  21.2 4.6 %fusion = bf16[12,1536,128]{2,0,1:T(8,128)(2,1)S(1)} fusion(bf16[512,12,128]{2,1,0:T(8,128)(2,1)} %copy.29, bf16[512,12,128]{2,1,0:T(8,128)(2,1)} %copy.28, bf16[512,12,128]{2,1,0:T(8,128)(2,1)} %copy.27, s32[12]{0:T(128)S(1)} %bitcast.49), kind=kOutput, calls=%fused_computation.1 | convolution fusion | flops 70779024 | bytes 9437232 | tf_op jit(solution)/shard_map/lbk,bj->ljk/dot_general | solution.py:9
  25.8 1.2 copy.38
  27.1 2.2 %copy-done.1 = bf16[12,1536,128]{2,1,0:T(8,128)(2,1)} copy-done((bf16[12,1536,128]{2,1,0:T(8,128)(2,1)}, bf16[12,1536,128]{2,1,0:T(8,128)(2,1)S(1)}, u32[]{:S(2)}) %copy-start.1) | copy-done | bytes 4718616
  29.4 0.7 copy.31
  30.1 5.1 %slice_convert_fusion = f32[1024,12,128]{2,0,1:T(8,128)} fusion(bf16[1536,12,128]{2,0,1:T(8,128)(2,1)} %bitcast.38), kind=kLoop, calls=%fused_computation.14 | loop fusion | flops 1572864 | bytes 9437184 | tf_op jit(solution)/shard_map/convert_element_type | solution.py:53
  35.3 6.6 %copy.32 = f32[1024,12,128]{0,2,1:T(8,128)} copy(f32[1024,12,128]{2,0,1:T(8,128)} %slice_convert_fusion) | data formatting | bytes 12582912 | tf_op jit(solution)/shard_map/convert_element_type | solution.py:53
  41.9 6.7 %copy.33 = f32[1024,1536]{1,0:T(8,128)} copy(f32[1024,1536]{0,1:T(8,128)} %bitcast.36) | data formatting | bytes 12582912 | tf_op jit(solution)/shard_map/convert_element_type | solution.py:53
  48.6 4.5 %fusion.14 = f32[1024,1536]{1,0:T(8,128)} fusion(bf16[512,1536]{0,1:T(8,128)(2,1)S(1)} %bitcast.43, bf16[512,512]{1,0:T(8,128)(2,1)S(1)} %bitcast.47, bf16[512,512]{1,0:T(8,128)(2,1)S(1)} %bitcast.48), kind=kOutput, calls=%fused_computation.28 | convolution fusion | flops 1612709888 | bytes 8912896 | tf_op jit(solution)/shard_map/dot_general | solution.py:54
  53.0 35.5 %all-gather.2.cloned.1.call-done = bf16[1536,1280]{1,0:T(8,128)(2,1)} async-done(((bf16[96,1280]{1,0:T(8,128)(2,1)}), bf16[1536,1280]{1,0:T(8,128)(2,1)}) %all-gather.2.cloned.1.call-update) | async-done | bytes 3932176 | tf_op jit(solution)/shard_map/all_gather | solution.py:62
  88.6 4.5 %convolution_convert_fusion.1 = bf16[512,1280]{1,0:T(8,128)(2,1)S(1)} fusion(bf16[512,1536]{0,1:T(8,128)(2,1)S(1)} %bitcast.44, bf16[1536,1280]{1,0:T(8,128)(2,1)} %all-gather.2.cloned.1.call-done), kind=kOutput, calls=%fused_computation.16 | convolution fusion | flops 2013921280 | bytes 6815744 | tf_op jit(solution)/shard_map/dot_general | solution.py:63
  93.2 1.1 copy-done.2
  94.3 6.6 %convolution_convert_fusion = bf16[1024,1280]{1,0:T(8,128)(2,1)S(1)} fusion(bf16[1536,1280]{1,0:T(8,128)(2,1)} %all-gather.2.cloned.1.call-done, f32[1024,1536]{1,0:T(8,128)S(1)} %copy-done, f32[1024,1536]{1,0:T(8,128)S(1)} %copy-done.2), kind=kOutput, calls=%fused_computation.12 | convolution fusion | flops 4032561152 | bytes 19136512 | tf_op jit(solution)/shard_map/dot_general | solution.py:64
  100.9 1.2 broadcast_select_fusion
  102.1 1.6 pad_maximum_fusion.1
  105.8 1.8 pad_maximum_fusion
  108.3 0.6 copy-done.5
  108.9 2.4 %fusion.9 = f32[1024,1024]{1,0:T(8,128)S(1)} fusion(bf16[512,1024]{1,0:T(8,128)(2,1)S(1)} %get-tuple-element.9, bf16[512,1024]{1,0:T(8,128)(2,1)S(1)} %copy-done.5, bf16[512,1024]{1,0:T(8,128)(2,1)S(1)} %slice.92, bf16[512,1024]{1,0:T(8,128)(2,1)S(1)} %get-tuple-element.8), kind=kOutput, calls=%fused_computation.23 | convolution fusion | flops 2155872256 | bytes 8388608 | tf_op jit(solution)/shard_map/dot_general | solution.py:19
  111.3 2.6 %add_convert_fusion.2 = bf16[1024,1024]{1,0:T(8,128)(2,1)S(1)} fusion(f32[1024,1024]{1,0:T(8,128)S(1)} %fusion.9, bf16[512,1024]{1,0:T(8,128)(2,1)S(1)} %get-tuple-element.9, bf16[512,1024]{1,0:T(8,128)(2,1)S(1)} %copy-done.5, bf16[512,1024]{1,0:T(8,128)(2,1)S(1)} %slice.92, bf16[512,1024]{1,0:T(8,128)(2,1)S(1)} %get-tuple-element.8), kind=kOutput, calls=%fused_computation.11 | convolution fusion | flops 2157969408 | bytes 10485760 | tf_op jit(solution)/shard_map/dot_general | solution.py:19
  113.9 2.2 %convert_element_type.46 = bf16[256,4,1024]{2,1,0:T(4,128)(2,1)} reshape(bf16[1024,1024]{1,0:T(8,128)(2,1)S(1)} %add_convert_fusion.2) | data formatting | bytes 4194304 | tf_op jit(solution)/shard_map/convert_element_type | solution.py:102
  116.1 9.8 %all-to-all-start = ((bf16[256,4,1024]{2,1,0:T(4,128)(2,1)}), bf16[256,4,1024]{2,1,0:T(4,128)(2,1)S(1)}, u32[]{:S(2)}, u32[]{:S(2)}) async-start(bf16[256,4,1024]{2,1,0:T(4,128)(2,1)} %convert_element_type.46), calls=%async_computation.1 | async-start | bytes 4194304 | tf_op jit(solution)/shard_map/all_to_all | solution.py:101
  125.9 5.8 %fusion.7 = f32[1024,256]{1,0:T(8,128)S(1)} fusion(f32[1024,1536]{1,0:T(8,128)} %fusion.14, f32[1024,1536]{1,0:T(8,128)} %copy.33, bf16[1536,1280]{1,0:T(8,128)(2,1)} %all-gather.2.cloned.1.call-done), kind=kOutput, calls=%fused_computation.13 | convolution fusion | flops 808452096 | bytes 14417920 | tf_op jit(solution)/shard_map/dot_general | solution.py:65
  131.7 1.0 slice_bitcast_fusion
  132.8 71.7 %reduce-scatter.2.cloned.1.call-done = f32[16,2560]{1,0:T(8,128)} async-done(((f32[256,2560]{1,0:T(8,128)}), f32[16,2560]{1,0:T(8,128)}) %reduce-scatter.2.cloned.1.call-update) | async-done | bytes 163856 | tf_op jit(solution)/shard_map/reduce_scatter | solution.py:83
  204.5 1.6 slice_bitcast_fusion.2
  206.1 0.8 convert_reduce_fusion
  (30 shorter events, 3.7 us)
Async XLA Ops:
  7.2 81.4 %all-gather.2.cloned.1.call-start = ((), (), s32[]{:S(2)}) async-start(), calls=%async_computation.2 | async-start | bytes 4177920 | tf_op jit(solution)/shard_map/all_gather | solution.py:62
  8.9 195.6 %reduce-scatter.2.cloned.1.call-start = ((), (), s32[]{:S(2)}) async-start(), calls=%async_computation.3 | async-start | bytes 2785280 | tf_op jit(solution)/shard_map/reduce_scatter | solution.py:83
  10.7 3.0 %copy-start.3 = (bf16[1,512,1536]{2,1,0:T(8,128)(2,1)S(1)}, bf16[1,512,1536]{2,1,0:T(8,128)(2,1)}, u32[]{:S(2)}) copy-start(bf16[1,512,1536]{2,1,0:T(8,128)(2,1)} %param.10) | copy-start | bytes 4718596
  14.4 3.0 %copy-start.4 = (bf16[1,512,1536]{2,1,0:T(8,128)(2,1)S(1)}, bf16[1,512,1536]{2,1,0:T(8,128)(2,1)}, u32[]{:S(2)}) copy-start(bf16[1,512,1536]{2,1,0:T(8,128)(2,1)} %param.12) | copy-start | bytes 4718596
  18.2 3.0 %copy-start.8 = (s32[1,12]{1,0:T(1,128)S(1)}, s32[1,12]{1,0:T(1,128)}, u32[]{:S(2)}) copy-start(s32[1,12]{1,0:T(1,128)} %param.13) | copy-start | bytes 148
  27.1 2.2 %copy-start.1 = (bf16[12,1536,128]{2,1,0:T(8,128)(2,1)}, bf16[12,1536,128]{2,1,0:T(8,128)(2,1)S(1)}, u32[]{:S(2)}) copy-start(bf16[12,1536,128]{2,1,0:T(8,128)(2,1)S(1)} %copy.38) | copy-start | bytes 14155780
  41.9 6.7 %copy-start.6 = (bf16[1,512,512]{2,1,0:T(8,128)(2,1)S(1)}, bf16[1,512,512]{2,1,0:T(8,128)(2,1)}, u32[]{:S(2)}) copy-start(bf16[1,512,512]{2,1,0:T(8,128)(2,1)} %param.9) | copy-start | bytes 1572868
  41.9 6.7 %copy-start.7 = (bf16[1,512,512]{2,1,0:T(8,128)(2,1)S(1)}, bf16[1,512,512]{2,1,0:T(8,128)(2,1)}, u32[]{:S(2)}) copy-start(bf16[1,512,512]{2,1,0:T(8,128)(2,1)} %param.8) | copy-start | bytes 1572868
  88.5 4.7 %copy-start = (f32[1024,1536]{1,0:T(8,128)S(1)}, f32[1024,1536]{1,0:T(8,128)}, u32[]{:S(2)}) copy-start(f32[1024,1536]{1,0:T(8,128)} %copy.33) | copy-start | bytes 18874372
  88.5 5.8 %copy-start.2 = (f32[1024,1536]{1,0:T(8,128)S(1)}, f32[1024,1536]{1,0:T(8,128)}, u32[]{:S(2)}) copy-start(f32[1024,1536]{1,0:T(8,128)} %fusion.14) | copy-start | bytes 18874372
  103.7 4.4 %collective-permute-start = (bf16[1024,1024]{1,0:T(8,128)(2,1)}, bf16[1024,1024]{1,0:T(8,128)(2,1)S(1)}, u32[]{:S(2)}, u32[]{:S(2)}) collective-permute-start(bf16[1024,1024]{1,0:T(8,128)(2,1)} %pad_maximum_fusion.1), channel_id=1, source_target_pairs={{0,16},{16,0},{32,48},{48,32},{64,80},{80,64},{96,112},{112,96},{1... | collective-permute-start | bytes 6291464 | tf_op jit(solution)/shard_map/ppermute | solution.py:93
  107.7 1.2 copy-start.5
  116.1 90.0 %all-to-all-start = ((bf16[256,4,1024]{2,1,0:T(4,128)(2,1)}), bf16[256,4,1024]{2,1,0:T(4,128)(2,1)S(1)}, u32[]{:S(2)}, u32[]{:S(2)}) async-start(bf16[256,4,1024]{2,1,0:T(4,128)(2,1)} %convert_element_type.46), calls=%async_computation.1 | async-start | bytes 4194304 | tf_op jit(solution)/shard_map/all_to_all | solution.py:101
Sparse Core Ops, SparseCore 0:
  10.3 78.1 all-gather.1
  107.8 96.6 reduce-scatter.1
where the time goes:
time: 215 us; the launch traced here: 214 us
  waiting for transfers between devices  108 us (50%)
  local copies, waits for them, and re-layouts  37.3 us (17%)
  matrix products  33.1 us (15%)
  between operations  14.2 us (7%)
  other arithmetic  12.2 us (6%)
  starting transfers between devices  9.88 us (5%)
    reduce_scatter x1, waiting for transfers between devices, body(): lax.psum_scatter(projected_rows(jnp.int32(0), mode_count, 0), 'leaf', sca...  71.7 us
    all_gather x1, waiting for transfers between devices, body(): mode_basis = lax.all_gather(basis_rows, 'leaf', axis=0, tiled=True)  35.5 us
    convert_element_type x2, local copies, waits for them, and re-layouts, body(): sides = placed[leaf_order:].astype(jnp.float32)  13.3 us
    all_to_all x1, starting transfers between devices, body(): lax.all_to_all(root_rows.reshape(device_count, root_width // device_count...  9.79 us
    concatenate x3, local copies, waits for them, and re-layouts, body(): jnp.concatenate([leaf_modes[0], mass_coupling[0], damp_coupling[0]], axis=0)  9.08 us
    dot_general x6, matrix products, left_product(): lax.dot_general(first_operand, second_operand, (((0,), (0,)), ((), ())),...  7.12 us
    unnamed x21, local copies, waits for them, and re-layouts  7.11 us
    dot_general x1, matrix products, body(): jnp.dot(half_work, mode_basis, preferred_element_type=jnp.float32)  6.6 us
  transfers between devices with their start and end apart: 4, of which 3 were waited for; matrix products, arithmetic and copies ran while one was open for 29% of the time, Pallas kernels for 0%

commit v1 on v0

--- a/solution.py
+++ b/solution.py
@@ -59,7 +59,9 @@
     half_work = (0.5 * product + sides).astype(jnp.bfloat16)
     full_work = (product + sides).astype(jnp.bfloat16)
     basis_rows = jnp.concatenate([mid_modes[0], mid_constraint[0]], axis=1)
-    mode_basis = lax.all_gather(basis_rows, "leaf", axis=0, tiled=True)
+    mode_basis = jnp.concatenate(
+        lax.all_to_all(jnp.stack([basis_rows] * lax.axis_size("leaf")), "leaf", 0, 0), axis=0
+    )
     left_sum = jnp.dot(constraint, mode_basis, preferred_element_type=jnp.float32)
     right_sum = jnp.dot(half_work, mode_basis, preferred_element_type=jnp.float32)
     coupling = jnp.dot(full_work, mode_basis[:, :mode_count], preferred_element_type=jnp.float32)

time: 215 us -> 239 us (1.11)
  starting transfers between devices: 9.88 us -> 22.3 us
  waiting for transfers between devices: 108 us -> 116 us
    all_to_all x0 -> x1, waiting for transfers between devices: none -> 44.2 us  [body(): lax.all_to_all(jnp.stack([basis_rows] * lax.axis_size('leaf')), 'leaf', 0...]
    all_gather x1 -> x0, waiting for transfers between devices: 35.5 us -> none  [body(): mode_basis = lax.all_gather(basis_rows, 'leaf', axis=0, tiled=True)]
    all_to_all x0 -> x1, starting transfers between devices: none -> 9.76 us  [body(): lax.all_to_all(jnp.stack([basis_rows] * lax.axis_size('leaf')), 'leaf', 0...]
    all_to_all x1, starting transfers between devices: 9.79 us -> 12.5 us  [body(): lax.all_to_all(root_rows.reshape(device_count, root_width // device_count...]
    unnamed x21 -> x25, local copies, waits for them, and re-layouts: 7.11 us -> 5.52 us
  transfers between devices with their start and end apart: 4 -> 4, of which waited for: 3 -> 3; matrix products, arithmetic and copies ran while one was open for 29% -> 26% of each run, Pallas kernels for 0% -> 0%
where the time goes in v1:
time: 239 us; the launch traced here: 238 us
  waiting for transfers between devices  116 us (49%)
  local copies, waits for them, and re-layouts  38.7 us (16%)
  matrix products  35.3 us (15%)
  starting transfers between devices  22.3 us (9%)
  between operations  14.3 us (6%)
  other arithmetic  11.5 us (5%)
    reduce_scatter x1, waiting for transfers between devices, body(): lax.psum_scatter(projected_rows(jnp.int32(0), mode_count, 0), 'leaf', sca...  71.5 us
    all_to_all x1, waiting for transfers between devices, body(): lax.all_to_all(jnp.stack([basis_rows] * lax.axis_size('leaf')), 'leaf', 0...  44.2 us
    convert_element_type x2, local copies, waits for them, and re-layouts, body(): sides = placed[leaf_order:].astype(jnp.float32)  13.2 us
    all_to_all x1, starting transfers between devices, body(): lax.all_to_all(root_rows.reshape(device_count, root_width // device_count...  12.5 us
    all_to_all x1, starting transfers between devices, body(): lax.all_to_all(jnp.stack([basis_rows] * lax.axis_size('leaf')), 'leaf', 0...  9.76 us
    concatenate x3, local copies, waits for them, and re-layouts, body(): jnp.concatenate([leaf_modes[0], mass_coupling[0], damp_coupling[0]], axis=0)  9.02 us
    dot_general x6, matrix products, left_product(): lax.dot_general(first_operand, second_operand, (((0,), (0,)), ((), ())),...  7.12 us
    dot_general x1, matrix products, body(): jnp.dot(half_work, mode_basis, preferred_element_type=jnp.float32)  6.74 us
  transfers between devices with their start and end apart: 4, of which 3 were waited for; matrix products, arithmetic and copies ran while one was open for 26% of the time, Pallas kernels for 0%

profile of v1, /device:TPU:4, one launch (start us, length us, event | category | flops | bytes accessed | tf_op | source)
XLA Modules:
  0.0 238.1 jit_solution(16512868729608290500)
XLA Ops:
  7.2 0.9 pad_maximum_fusion.8
  8.1 2.2 stack.2
  10.4 9.8 %all-to-all-start = ((bf16[16,96,1280]{2,1,0:T(8,128)(2,1)}), bf16[16,96,1280]{2,1,0:T(8,128)(2,1)}, u32[]{:S(2)}, u32[]{:S(2)}) async-start(bf16[16,96,1280]{2,1,0:T(8,128)(2,1)} %stack.2), calls=%async_computation | async-start | bytes 7864320 | tf_op jit(solution)/shard_map/all_to_all | solution.py:63
  20.2 0.7 copy.26
  20.9 3.0 %copy.29 = bf16[512,12,128]{2,1,0:T(8,128)(2,1)} copy(bf16[512,12,128]{0,2,1:T(8,128)(2,1)S(1)} %bitcast.43) | data formatting | bytes 3145728 | tf_op jit(solution)/shard_map/concatenate | solution.py:47
  23.9 0.7 copy.25
  24.7 3.0 %copy.28 = bf16[512,12,128]{2,1,0:T(8,128)(2,1)} copy(bf16[512,12,128]{0,2,1:T(8,128)(2,1)S(1)} %bitcast.44) | data formatting | bytes 3145728 | tf_op jit(solution)/shard_map/concatenate | solution.py:47
  27.7 0.7 copy.24
  28.4 3.0 %copy.27 = bf16[512,12,128]{2,1,0:T(8,128)(2,1)} copy(bf16[512,12,128]{0,2,1:T(8,128)(2,1)S(1)} %bitcast.45) | data formatting | bytes 3145728 | tf_op jit(solution)/shard_map/concatenate | solution.py:47
  31.4 4.6 %fusion = bf16[12,1536,128]{2,0,1:T(8,128)(2,1)S(1)} fusion(bf16[512,12,128]{2,1,0:T(8,128)(2,1)} %copy.29, bf16[512,12,128]{2,1,0:T(8,128)(2,1)} %copy.28, bf16[512,12,128]{2,1,0:T(8,128)(2,1)} %copy.27, s32[12]{0:T(128)S(1)} %bitcast.52), kind=kOutput, calls=%fused_computation.1 | convolution fusion | flops 70779024 | bytes 9437232 | tf_op jit(solution)/shard_map/lbk,bj->ljk/dot_general | solution.py:9
  36.0 1.2 copy.38
  37.3 2.2 copy-done
  39.6 1.6 copy.31
  41.2 5.1 %slice_convert_fusion = f32[1024,12,128]{2,0,1:T(8,128)} fusion(bf16[1536,12,128]{2,0,1:T(8,128)(2,1)} %bitcast.41), kind=kLoop, calls=%fused_computation.14 | loop fusion | flops 1572864 | bytes 9437184 | tf_op jit(solution)/shard_map/convert_element_type | solution.py:53
  46.3 6.6 %copy.32 = f32[1024,12,128]{0,2,1:T(8,128)} copy(f32[1024,12,128]{2,0,1:T(8,128)} %slice_convert_fusion) | data formatting | bytes 12582912 | tf_op jit(solution)/shard_map/convert_element_type | solution.py:53
  52.9 6.7 %copy.33 = f32[1024,1536]{1,0:T(8,128)} copy(f32[1024,1536]{0,1:T(8,128)} %bitcast.39) | data formatting | bytes 12582912 | tf_op jit(solution)/shard_map/convert_element_type | solution.py:53
  59.6 6.0 %fusion.14 = f32[1024,1536]{1,0:T(8,128)} fusion(bf16[512,1536]{0,1:T(8,128)(2,1)} %bitcast.46, bf16[512,512]{1,0:T(8,128)(2,1)S(1)} %bitcast.50, bf16[512,512]{1,0:T(8,128)(2,1)S(1)} %bitcast.51), kind=kOutput, calls=%fused_computation.28 | convolution fusion | flops 1612709888 | bytes 8912896 | tf_op jit(solution)/shard_map/dot_general | solution.py:54
  65.6 44.2 %all-to-all-done = bf16[16,96,1280]{2,1,0:T(8,128)(2,1)} async-done(((bf16[16,96,1280]{2,1,0:T(8,128)(2,1)}), bf16[16,96,1280]{2,1,0:T(8,128)(2,1)}, u32[]{:S(2)}, u32[]{:S(2)}) %all-to-all-start) | async-done | bytes 3932192 | tf_op jit(solution)/shard_map/all_to_all | solution.py:63
  109.7 5.0 %convolution_convert_fusion.1 = bf16[512,1280]{1,0:T(8,128)(2,1)S(1)} fusion(bf16[512,1536]{0,1:T(8,128)(2,1)} %bitcast.47, bf16[1536,1280]{1,0:T(8,128)(2,1)} %bitcast.12), kind=kOutput, calls=%fused_computation.16 | convolution fusion | flops 2013921280 | bytes 6815744 | tf_op jit(solution)/shard_map/dot_general | solution.py:65
  115.4 6.7 %convolution_convert_fusion = bf16[1024,1280]{1,0:T(8,128)(2,1)S(1)} fusion(bf16[1536,1280]{1,0:T(8,128)(2,1)} %bitcast.12, f32[1024,1536]{1,0:T(8,128)S(1)} %bitcast.38, f32[1024,1536]{1,0:T(8,128)S(1)} %copy-done.1), kind=kOutput, calls=%fused_computation.12 | convolution fusion | flops 4032561152 | bytes 19136512 | tf_op jit(solution)/shard_map/dot_general | solution.py:66
  122.2 1.2 broadcast_select_fusion
  123.3 1.6 pad_maximum_fusion.1
  127.1 1.8 pad_maximum_fusion
  130.1 2.4 %fusion.9 = f32[1024,1024]{1,0:T(8,128)S(1)} fusion(bf16[512,1024]{1,0:T(8,128)(2,1)S(1)} %get-tuple-element.9, bf16[512,1024]{1,0:T(8,128)(2,1)S(1)} %copy-done.5, bf16[512,1024]{1,0:T(8,128)(2,1)S(1)} %slice.92, bf16[512,1024]{1,0:T(8,128)(2,1)S(1)} %get-tuple-element.8), kind=kOutput, calls=%fused_computation.23 | convolution fusion | flops 2155872256 | bytes 8388608 | tf_op jit(solution)/shard_map/dot_general | solution.py:19
  132.5 2.6 %add_convert_fusion.2 = bf16[1024,1024]{1,0:T(8,128)(2,1)S(1)} fusion(f32[1024,1024]{1,0:T(8,128)S(1)} %fusion.9, bf16[512,1024]{1,0:T(8,128)(2,1)S(1)} %get-tuple-element.9, bf16[512,1024]{1,0:T(8,128)(2,1)S(1)} %copy-done.5, bf16[512,1024]{1,0:T(8,128)(2,1)S(1)} %slice.92, bf16[512,1024]{1,0:T(8,128)(2,1)S(1)} %get-tuple-element.8), kind=kOutput, calls=%fused_computation.11 | convolution fusion | flops 2157969408 | bytes 10485760 | tf_op jit(solution)/shard_map/dot_general | solution.py:19
  135.1 2.2 convert_element_type.46
  137.4 12.5 %all-to-all-start.1 = ((bf16[256,4,1024]{2,1,0:T(4,128)(2,1)}), bf16[256,4,1024]{2,1,0:T(4,128)(2,1)S(1)}, u32[]{:S(2)}, u32[]{:S(2)}) async-start(bf16[256,4,1024]{2,1,0:T(4,128)(2,1)} %convert_element_type.46), calls=%async_computation.2 | async-start | bytes 4194304 | tf_op jit(solution)/shard_map/all_to_all | solution.py:103
  149.8 5.8 %fusion.7 = f32[1024,256]{1,0:T(8,128)S(1)} fusion(f32[1024,1536]{1,0:T(8,128)} %fusion.14, f32[1024,1536]{1,0:T(8,128)} %copy.33, bf16[1536,1280]{1,0:T(8,128)(2,1)} %bitcast.12), kind=kOutput, calls=%fused_computation.13 | convolution fusion | flops 808452096 | bytes 14417920 | tf_op jit(solution)/shard_map/dot_general | solution.py:67
  155.7 1.0 slice_bitcast_fusion
  156.7 71.5 %reduce-scatter.2.cloned.1.call-done = f32[16,2560]{1,0:T(8,128)} async-done(((f32[256,2560]{1,0:T(8,128)}), f32[16,2560]{1,0:T(8,128)}) %reduce-scatter.2.cloned.1.call-update) | async-done | bytes 163856 | tf_op jit(solution)/shard_map/reduce_scatter | solution.py:85
  228.2 1.6 slice_bitcast_fusion.2
  229.8 0.8 convert_reduce_fusion
  (35 shorter events, 4.8 us)
Async XLA Ops:
  10.4 9.8 %copy-start.2 = (bf16[1,512,1536]{2,1,0:T(8,128)(2,1)S(1)}, bf16[1,512,1536]{2,1,0:T(8,128)(2,1)}, u32[]{:S(2)}) copy-start(bf16[1,512,1536]{2,1,0:T(8,128)(2,1)} %param.11) | copy-start | bytes 4718596
  10.4 99.4 %all-to-all-start = ((bf16[16,96,1280]{2,1,0:T(8,128)(2,1)}), bf16[16,96,1280]{2,1,0:T(8,128)(2,1)}, u32[]{:S(2)}, u32[]{:S(2)}) async-start(bf16[16,96,1280]{2,1,0:T(8,128)(2,1)} %stack.2), calls=%async_computation | async-start | bytes 7864320 | tf_op jit(solution)/shard_map/all_to_all | solution.py:63
  20.1 208.1 %reduce-scatter.2.cloned.1.call-start = ((), (), s32[]{:S(2)}) async-start(), calls=%async_computation.3 | async-start | bytes 2785280 | tf_op jit(solution)/shard_map/reduce_scatter | solution.py:85
  20.9 3.0 %copy-start.3 = (bf16[1,512,1536]{2,1,0:T(8,128)(2,1)S(1)}, bf16[1,512,1536]{2,1,0:T(8,128)(2,1)}, u32[]{:S(2)}) copy-start(bf16[1,512,1536]{2,1,0:T(8,128)(2,1)} %param.10) | copy-start | bytes 4718596
  24.7 3.0 %copy-start.4 = (bf16[1,512,1536]{2,1,0:T(8,128)(2,1)S(1)}, bf16[1,512,1536]{2,1,0:T(8,128)(2,1)}, u32[]{:S(2)}) copy-start(bf16[1,512,1536]{2,1,0:T(8,128)(2,1)} %param.12) | copy-start | bytes 4718596
  28.4 3.0 %copy-start.8 = (s32[1,12]{1,0:T(1,128)S(1)}, s32[1,12]{1,0:T(1,128)}, u32[]{:S(2)}) copy-start(s32[1,12]{1,0:T(1,128)} %param.13) | copy-start | bytes 148
  37.3 2.2 copy-start
  52.9 6.7 %copy-start.6 = (bf16[1,512,512]{2,1,0:T(8,128)(2,1)S(1)}, bf16[1,512,512]{2,1,0:T(8,128)(2,1)}, u32[]{:S(2)}) copy-start(bf16[1,512,512]{2,1,0:T(8,128)(2,1)} %param.9) | copy-start | bytes 1572868
  52.9 6.7 %copy-start.7 = (bf16[1,512,512]{2,1,0:T(8,128)(2,1)S(1)}, bf16[1,512,512]{2,1,0:T(8,128)(2,1)}, u32[]{:S(2)}) copy-start(bf16[1,512,512]{2,1,0:T(8,128)(2,1)} %param.8) | copy-start | bytes 1572868
  59.6 55.3 %slice-start = ((s8[6291456]{0:T(1024)(128)(4,1)}), s8[2097152]{0:T(1024)(128)(4,1)S(1)}, s32[]{:S(2)}) async-start(s8[6291456]{0:T(1024)(128)(4,1)} %bitcast.37), calls=%async_computation.4 | async-start | bytes 4194304
  109.7 5.2 %slice-start.1 = ((s8[6291456]{0:T(1024)(128)(4,1)}), s8[4194304]{0:T(1024)(128)(4,1)S(1)}, s32[]{:S(2)}) async-start(s8[6291456]{0:T(1024)(128)(4,1)} %bitcast.37), calls=%async_computation.5 | async-start | bytes 8388608
  109.7 5.7 %copy-start.1 = (f32[1024,1536]{1,0:T(8,128)S(1)}, f32[1024,1536]{1,0:T(8,128)}, u32[]{:S(2)}) copy-start(f32[1024,1536]{1,0:T(8,128)} %fusion.14) | copy-start | bytes 18874372
  124.9 4.4 %collective-permute-start = (bf16[1024,1024]{1,0:T(8,128)(2,1)}, bf16[1024,1024]{1,0:T(8,128)(2,1)S(1)}, u32[]{:S(2)}, u32[]{:S(2)}) collective-permute-start(bf16[1024,1024]{1,0:T(8,128)(2,1)} %pad_maximum_fusion.1), channel_id=1, source_target_pairs={{0,16},{16,0},{32,48},{48,32},{64,80},{80,64},{96,112},{112,96},{1... | collective-permute-start | bytes 6291464 | tf_op jit(solution)/shard_map/ppermute | solution.py:95
  128.9 1.2 copy-start.5
  137.4 92.4 %all-to-all-start.1 = ((bf16[256,4,1024]{2,1,0:T(4,128)(2,1)}), bf16[256,4,1024]{2,1,0:T(4,128)(2,1)S(1)}, u32[]{:S(2)}, u32[]{:S(2)}) async-start(bf16[256,4,1024]{2,1,0:T(4,128)(2,1)} %convert_element_type.46), calls=%async_computation.2 | async-start | bytes 4194304 | tf_op jit(solution)/shard_map/all_to_all | solution.py:103
Sparse Core Ops, SparseCore 0:
  129.0 99.1 reduce-scatter.1
